TPU v7x, 32 devices: a whole 2x2x4 slice. The times are simulated.
32 devices in a mesh: dom: 8 (over z, x), grp: 4 (over y, core).
Axes of the slice: x: 2, y: 2, z: 4, core: 2. Of those that a mesh axis runs over, the one named last changes fastest.
Arguments:
- x_current: bfloat16 [131072, 128], P(('dom', 'grp')), may hold values from -6 to 6
- x_cached: bfloat16 [131072, 128], P(('dom', 'grp')), may hold values from -6 to 6
- w_self: bfloat16 [128, 512], replicated, may hold values from -0.5 to 0.5
- w_neigh: bfloat16 [128, 512], replicated, may hold values from -1 to 1
- bias: float32 [512], replicated, may hold values from -3 to 3
- tile_columns: int32 [1024, 40], P(('dom', 'grp')), may hold values from 0 to 159
- tile_count: int32 [1024], P(('dom', 'grp')), may hold values from 1 to 40, as said below
- adjacency: int32 [1024, 40, 2048], P(('dom', 'grp')), may hold values from 0 to 255, as said below
- degree: int32 [131072], P(('dom', 'grp')), may hold values from 1 to 5128, as said below
- boundary_blocks: int32 [32, 1], P(('dom', 'grp')), may hold values from 0 to 31
Outputs:
- hidden: bfloat16 [131072, 512], P(('dom', 'grp'))
Inputs may be any that keep to these rules, and one draw needn't show every extreme that they name: `tile_count`: every device has a row block with all 40 slots live. `adjacency`: 8 entries of a tile row packed into each word, bit b for column 8 c + b. `degree`: at least the number of ones in the row of the live tiles of the node's row block.
All inputs are finite; a program needn't handle non-finite values.
Results may differ from a plain program's by a relative error of at most 0.0025.
Values may be sent and summed in bfloat16 or wider, within the bound.
No kernel may reach another device: no remote copies, remote signals or barrier semaphores. Data moves between devices by JAX's collectives and lax.ppermute only.
A program may use at most 192 MiB of HBM per device.

v0:
```python
import functools

import jax
import jax.numpy as jnp
from jax import lax
from jax.experimental import pallas as pl
from jax.experimental.pallas import tpu as pltpu
from jax.sharding import PartitionSpec as P

CHUNK = 8


def _layer_kernel(cols_ref, counts_ref, grp_ref, adj_ref, xc_ref, deg_ref, ws_ref, wn_ref, b_ref,
                  *rest, per_tile, tile, n_table, n_grp, dev_blocks):
    pieces = rest[:n_grp + 1]
    out_ref, table_ref, sems, words_ref, acc_ref, mexp_ref, perm_ref, pick_ref = rest[n_grp + 1:]
    r = pl.program_id(0)
    count = counts_ref[r]
    g = grp_ref[0]
    part = n_grp * dev_blocks

    @pl.when(r == 0)
    def _():
        rows = lax.broadcasted_iota(jnp.int32, (tile, 8 * tile), 0)
        cols = lax.broadcasted_iota(jnp.int32, (tile, 8 * tile), 1)
        jj = cols % tile
        hit = rows == (tile // 8) * (cols // tile) + jj // 8
        scale = lax.shift_left(jnp.ones_like(jj), 7 - jj % 8).astype(jnp.float32)
        mexp_ref[...] = jnp.where(hit, scale, 0.0).astype(jnp.bfloat16)
        ri = lax.broadcasted_iota(jnp.int32, (tile, tile), 0)
        ci = lax.broadcasted_iota(jnp.int32, (tile, tile), 1)
        kq = tile // 8
        perm_ref[...] = (ri == 8 * (ci % kq) + ci // kq).astype(jnp.bfloat16)
        pick_ref[...] = (ci == 8 * (ri % kq) + ri // kq).astype(jnp.float32)
        copies = []
        for d in range(n_grp):
            copies.append(pltpu.make_async_copy(
                pieces[d], table_ref.at[pl.ds(d * dev_blocks, dev_blocks)], sems.at[d]))
        n_halo = n_table - part
        copies.append(pltpu.make_async_copy(
            pieces[n_grp], table_ref.at[pl.ds(part, n_halo)], sems.at[n_grp]))
        for cp in copies:
            cp.start()
        for cp in copies:
            cp.wait()

    kk = tile // 8
    for k in range(kk):
        words_ref[pl.ds(k * per_tile, per_tile), :] = adj_ref[0, :, pl.ds(k * tile, tile)]
    acc_ref[...] = jnp.zeros_like(acc_ref)

    def chunk(c, masked):
            words = jnp.concatenate(
                [words_ref[pl.ds(c * CHUNK + tl, kk, stride=per_tile), :] for tl in range(CHUNK)],
                axis=0)
            spread = jnp.dot(words.astype(jnp.bfloat16), mexp_ref[...],
                             preferred_element_type=jnp.float32)
            bits = (spread.astype(jnp.int32) & 128).astype(jnp.bfloat16)
            rows = []
            for s in range(8):
                rows.append(jnp.concatenate(
                    [bits[tl * kk:(tl + 1) * kk, s * tile:(s + 1) * tile] for tl in range(CHUNK)],
                    axis=1))
            a_cat = jnp.concatenate(rows, axis=0)
            xs = []
            for tl in range(CHUNK):
                t = c * CHUNK + tl
                col = cols_ref[r, t]
                if n_grp == 4:
                    slot = jnp.bitwise_xor(col // dev_blocks, g)
                else:
                    slot = (g - col // dev_blocks + n_grp) % n_grp
                rel = slot * dev_blocks + col % dev_blocks
                col = jnp.clip(jnp.where(col < part, rel, col), 0, n_table - 1)
                xt = table_ref[col]
                if masked:
                    xt = jnp.where(t < count, xt, jnp.zeros_like(xt))
                xs.append(xt)
            x_cat = jnp.concatenate(xs, axis=0)
            acc_ref[...] += jnp.dot(a_cat, x_cat, preferred_element_type=jnp.float32)

    for c in range(per_tile // CHUNK):
        pl.when((c + 1) * CHUNK <= count)(functools.partial(chunk, c, False))
        pl.when((c * CHUNK < count) & (count < (c + 1) * CHUNK))(functools.partial(chunk, c, True))

    acc = acc_ref[...]
    totals = acc * (1.0 / 128.0)
    deg_row = deg_ref[pl.ds(r, 1), :].astype(jnp.float32)
    deg_perm = jnp.sum(pick_ref[...] * deg_row, axis=1, keepdims=True)
    avg_perm = (totals / deg_perm).astype(jnp.bfloat16)
    avg = jnp.dot(perm_ref[...], avg_perm, preferred_element_type=jnp.float32).astype(jnp.bfloat16)
    summed = (jnp.dot(xc_ref[...], ws_ref[...], preferred_element_type=jnp.float32)
              + jnp.dot(avg, wn_ref[...], preferred_element_type=jnp.float32) + b_ref[...])
    out_ref[...] = jnp.maximum(summed, 0.0).astype(out_ref.dtype)


def on_device(
    x_current,
    x_cached,
    w_self,
    w_neigh,
    bias,
    tile_columns,
    tile_count,
    adjacency,
    degree,
    boundary_blocks,
):
    node_rows, width = x_current.shape
    row_blocks, per_tile = tile_columns.shape
    tile_rows = node_rows // row_blocks
    hidden = w_self.shape[1]
    kk = tile_rows // 8
    assert per_tile % CHUNK == 0
    n_grp = lax.psum(1, "grp")
    chosen = x_cached.reshape(row_blocks, tile_rows, width)[boundary_blocks[0]]
    n_dom = lax.psum(1, "dom")
    n_dev = n_dom * n_grp
    spread_out = jnp.broadcast_to(chosen[None], (n_dev,) + chosen.shape).reshape(
        (n_dev * chosen.shape[0],) + chosen.shape[1:])
    halo_blocks = lax.all_to_all(spread_out, ("dom", "grp"), 0, 0, tiled=True)
    own_blocks = x_current.reshape(row_blocks, tile_rows, width)
    pieces = [own_blocks]
    if n_grp == 4:
        near = lax.ppermute(own_blocks, "grp", [(i, i ^ 1) for i in range(4)])
        far = lax.ppermute(own_blocks, "grp", [(i, i ^ 2) for i in range(4)])
        far_near = lax.ppermute(far, "grp", [(i, i ^ 1) for i in range(4)])
        pieces += [near, far, far_near]
    else:
        for d in range(1, n_grp):
            pieces.append(lax.ppermute(own_blocks, "grp", [(i, (i + d) % n_grp) for i in range(n_grp)]))
    pieces.append(halo_blocks)
    n_table = n_grp * row_blocks + halo_blocks.shape[0]
    grp_idx = jnp.stack([lax.axis_index("grp"), lax.axis_index("grp")]).astype(jnp.int32)

    deg = degree.reshape(row_blocks, tile_rows)
    b2 = bias.reshape(1, hidden)

    kernel = functools.partial(_layer_kernel, per_tile=per_tile, tile=tile_rows, n_table=n_table,
                               n_grp=n_grp, dev_blocks=row_blocks)
    grid_spec = pltpu.PrefetchScalarGridSpec(
        num_scalar_prefetch=3,
        grid=(row_blocks,),
        in_specs=[
            pl.BlockSpec((1, per_tile, tile_rows * kk), lambda r, *_: (r, 0, 0)),
            pl.BlockSpec((tile_rows, width), lambda r, *_: (r, 0)),
            pl.BlockSpec((row_blocks, tile_rows), lambda r, *_: (0, 0)),
            pl.BlockSpec((width, hidden), lambda r, *_: (0, 0)),
            pl.BlockSpec((width, hidden), lambda r, *_: (0, 0)),
            pl.BlockSpec((1, hidden), lambda r, *_: (0, 0)),
        ] + [pl.BlockSpec(memory_space=pl.ANY)] * (n_grp + 1),
        out_specs=pl.BlockSpec((tile_rows, hidden), lambda r, *_: (r, 0)),
        scratch_shapes=[pltpu.VMEM((n_table, tile_rows, width), jnp.bfloat16),
                        pltpu.SemaphoreType.DMA((n_grp + 1,)),
                        pltpu.VMEM((per_tile * kk, tile_rows), jnp.int32),
                        pltpu.VMEM((tile_rows, width), jnp.float32),
                        pltpu.VMEM((tile_rows, 8 * tile_rows), jnp.bfloat16),
                        pltpu.VMEM((tile_rows, tile_rows), jnp.bfloat16),
                        pltpu.VMEM((tile_rows, tile_rows), jnp.float32)],
    )
    return pl.pallas_call(
        kernel,
        grid_spec=grid_spec,
        out_shape=jax.ShapeDtypeStruct((node_rows, hidden), jnp.bfloat16),
        compiler_params=pltpu.CompilerParams(
            dimension_semantics=("arbitrary",), vmem_limit_bytes=48 * 1024 * 1024),
    )(*[pltpu.with_memory_space_constraint(a, pltpu.HBM) for a in
        (tile_columns, tile_count, grp_idx, adjacency, x_current, deg, w_self, w_neigh, b2)], *pieces)


def solution(mesh):
    in_specs = (
        P(("dom", "grp"), None),
        P(("dom", "grp"), None),
        P(),
        P(),
        P(),
        P(("dom", "grp"), None),
        P(("dom", "grp")),
        P(("dom", "grp"), None, None),
        P(("dom", "grp")),
        P(("dom", "grp"), None),
    )
    out_specs = P(("dom", "grp"), None)
    return jax.shard_map(
        on_device, mesh=mesh, in_specs=in_specs, out_specs=out_specs, check_vma=False
    )
```

profile of v0, /device:TPU:7, one launch (start us, length us, event | category | flops | bytes accessed | tf_op | source)
XLA Modules:
  0.0 107.3 jit_solution(11547421663893484523)
XLA Ops:
  0.0 0.0 copy-start
  0.0 0.2 collective-permute-start.1
  1.0 0.3 copy-done
  1.2 1.2 %reshape.22 = bf16[32,128,128]{2,1,0:T(8,128)(2,1)} broadcast(bf16[128,128]{1,0:T(8,128)(2,1)S(1)} %dynamic-slice_bitcast_fusion), dimensions={1,2} | broadcast | bytes 1081344 | tf_op jit(solution)/shard_map/reshape | solution.py:119
  2.4 6.4 %all-to-all-start = ((bf16[32,128,128]{2,1,0:T(8,128)(2,1)}), bf16[32,128,128]{2,1,0:T(8,128)(2,1)S(1)}, u32[]{:S(2)}, u32[]{:S(2)}) async-start(bf16[32,128,128]{2,1,0:T(8,128)(2,1)} %reshape.22), calls=%async_computation | async-start | bytes 2097152 | tf_op jit(solution)/shard_map/all_to_all | solution.py:121
  8.8 0.5 collective-permute-start
  9.3 24.8 %collective-permute-done.1.rest_2_ = bf16[32,128,128]{2,1,0:T(8,128)(2,1)S(1)} collective-permute-done((bf16[32,128,128]{2,1,0:T(8,128)(2,1)}, bf16[32,128,128]{2,1,0:T(8,128)(2,1)S(1)}, u32[]{:S(2)}, u32[]{:S(2)}) %collective-permute-start.1) | collective-permute-done | bytes 1048608 | tf_op jit(solution)/shard_map/ppermute | solution.py:126
  34.1 2.2 %collective-permute-start.2 = (bf16[32,128,128]{2,1,0:T(8,128)(2,1)S(1)}, bf16[32,128,128]{2,1,0:T(8,128)(2,1)}, u32[]{:S(2)}, u32[]{:S(2)}) collective-permute-start(bf16[32,128,128]{2,1,0:T(8,128)(2,1)S(1)} %collective-permute-done.1.rest_2_), channel_id=1, source_target_pairs={{0,1},{1,0},{2,3},{3,2},{4,5},{5,4},{6,7},{7,6},{8,9},{9,8},{10,11... | collective-permute-start | bytes 3145736 | tf_op jit(solution)/shard_map/ppermute | solution.py:127
  36.3 0.6 pad_add_fusion.grp_ref
  36.9 0.0 collective-permute-done.rest_1_
  36.9 0.0 all-to-all-done.rest_4_
  36.9 1.8 %collective-permute-done.2.rest_3_ = bf16[32,128,128]{2,1,0:T(8,128)(2,1)} collective-permute-done((bf16[32,128,128]{2,1,0:T(8,128)(2,1)S(1)}, bf16[32,128,128]{2,1,0:T(8,128)(2,1)}, u32[]{:S(2)}, u32[]{:S(2)}) %collective-permute-start.2) | collective-permute-done | bytes 1048608 | tf_op jit(solution)/shard_map/ppermute | solution.py:127
  38.7 68.5 %shard_map.100 = bf16[4096,512]{1,0:T(8,128)(2,1)} custom-call(s32[32,40]{1,0:T(8,128)} %cols_ref.1, s32[32]{0:T(128)} %counts_ref.1, s32[2]{0:T(128)} %pad_add_fusion.grp_ref, s32[32,40,2048]{2,1,0:T(8,128)} %adj_ref.1, bf16[4096,128]{1,0:T(8,128)(2,1)} %xc_ref.1, s32[32,128]{1,0:T(8,128)} %bitcast.16, bf16[128,512]{1,0:T(8,128)(2,1)} %ws_ref.1, ...), custom_call_target="tpu_custom_call" | custom-call | tf_op jit(solution)/shard_map/pallas_call | solution.py:161
  (1 shorter events, 0.0 us)
Async XLA Ops:
  0.0 1.2 %copy-start = (bf16[4096,128]{1,0:T(8,128)(2,1)S(1)}, bf16[4096,128]{1,0:T(8,128)(2,1)}, u32[]{:S(2)}) copy-start(bf16[4096,128]{1,0:T(8,128)(2,1)} %param.11) | copy-start | bytes 3145732
  0.0 34.1 %collective-permute-start.1 = (bf16[32,128,128]{2,1,0:T(8,128)(2,1)}, bf16[32,128,128]{2,1,0:T(8,128)(2,1)S(1)}, u32[]{:S(2)}, u32[]{:S(2)}) collective-permute-start(bf16[32,128,128]{2,1,0:T(8,128)(2,1)} %bitcast.13), channel_id=1, source_target_pairs={{0,2},{1,3},{2,0},{3,1},{4,6},{5,7},{6,4},{7,5},{8,10},{9,11},{10,... | collective-permute-start | bytes 3145736 | tf_op jit(solution)/shard_map/ppermute | solution.py:126
  2.4 34.5 %all-to-all-start = ((bf16[32,128,128]{2,1,0:T(8,128)(2,1)}), bf16[32,128,128]{2,1,0:T(8,128)(2,1)S(1)}, u32[]{:S(2)}, u32[]{:S(2)}) async-start(bf16[32,128,128]{2,1,0:T(8,128)(2,1)} %reshape.22), calls=%async_computation | async-start | bytes 2097152 | tf_op jit(solution)/shard_map/all_to_all | solution.py:121
  8.8 28.1 %collective-permute-start = (bf16[32,128,128]{2,1,0:T(8,128)(2,1)}, bf16[32,128,128]{2,1,0:T(8,128)(2,1)}, u32[]{:S(2)}, u32[]{:S(2)}) collective-permute-start(bf16[32,128,128]{2,1,0:T(8,128)(2,1)} %bitcast.14), channel_id=1, source_target_pairs={{0,1},{1,0},{2,3},{3,2},{4,5},{5,4},{6,7},{7,6},{8,9},{9,8},{10,11... | collective-permute-start | bytes 3145736 | tf_op jit(solution)/shard_map/ppermute | solution.py:125
  34.1 4.7 %collective-permute-start.2 = (bf16[32,128,128]{2,1,0:T(8,128)(2,1)S(1)}, bf16[32,128,128]{2,1,0:T(8,128)(2,1)}, u32[]{:S(2)}, u32[]{:S(2)}) collective-permute-start(bf16[32,128,128]{2,1,0:T(8,128)(2,1)S(1)} %collective-permute-done.1.rest_2_), channel_id=1, source_target_pairs={{0,1},{1,0},{2,3},{3,2},{4,5},{5,4},{6,7},{7,6},{8,9},{9,8},{10,11... | collective-permute-start | bytes 3145736 | tf_op jit(solution)/shard_map/ppermute | solution.py:127
where the time goes:
time: 108 us; the launch traced here: 107 us
  Pallas kernels  68.5 us (63%)
  waiting for transfers between devices  26.6 us (25%)
  starting transfers between devices  9.29 us (9%)
  local copies, waits for them, and re-layouts  1.47 us (1%)
    pallas_call x1, Pallas kernels, on_device(): pl.pallas_call(kernel, grid_spec=grid_spec, out_shape=jax.ShapeDtypeStruc...  68.5 us
    ppermute x1, waiting for transfers between devices, on_device(): far = lax.ppermute(own_blocks, 'grp', [(i, i ^ 2) for i in range(4)])  24.8 us
    all_to_all x1, starting transfers between devices, on_device(): halo_blocks = lax.all_to_all(spread_out, ('dom', 'grp'), 0, 0, tiled=True)  6.37 us
    ppermute x1, starting transfers between devices, on_device(): far_near = lax.ppermute(far, 'grp', [(i, i ^ 1) for i in range(4)])  2.23 us
  transfers between devices with their start and end apart: 4, of which 2 were waited for; matrix products, arithmetic and copies ran while one was open for 2% of the time, Pallas kernels for 0%

commit v1 on v0

--- a/solution.py
+++ b/solution.py
@@ -10,14 +10,10 @@
 CHUNK = 8
 
 
-def _layer_kernel(cols_ref, counts_ref, grp_ref, adj_ref, xc_ref, deg_ref, ws_ref, wn_ref, b_ref,
-                  *rest, per_tile, tile, n_table, n_grp, dev_blocks):
-    pieces = rest[:n_grp + 1]
-    out_ref, table_ref, sems, words_ref, acc_ref, mexp_ref, perm_ref, pick_ref = rest[n_grp + 1:]
+def _bits_kernel(counts_ref, adj_ref, out_ref, words_ref, mexp_ref, *, per_tile, tile):
     r = pl.program_id(0)
     count = counts_ref[r]
-    g = grp_ref[0]
-    part = n_grp * dev_blocks
+    kk = tile // 8
 
     @pl.when(r == 0)
     def _():
@@ -27,6 +23,38 @@
         hit = rows == (tile // 8) * (cols // tile) + jj // 8
         scale = lax.shift_left(jnp.ones_like(jj), 7 - jj % 8).astype(jnp.float32)
         mexp_ref[...] = jnp.where(hit, scale, 0.0).astype(jnp.bfloat16)
+
+    for k in range(kk):
+        words_ref[pl.ds(k * per_tile, per_tile), :] = adj_ref[0, :, pl.ds(k * tile, tile)]
+
+    for c in range(per_tile // CHUNK):
+        @pl.when(c * CHUNK < count)
+        def _():
+            words = jnp.concatenate(
+                [words_ref[pl.ds(c * CHUNK + tl, kk, stride=per_tile), :] for tl in range(CHUNK)],
+                axis=0)
+            spread = jnp.dot(words.astype(jnp.bfloat16), mexp_ref[...],
+                             preferred_element_type=jnp.float32)
+            bits = (spread.astype(jnp.int32) & 128).astype(jnp.bfloat16)
+            rows = []
+            for s in range(8):
+                rows.append(jnp.concatenate(
+                    [bits[tl * kk:(tl + 1) * kk, s * tile:(s + 1) * tile] for tl in range(CHUNK)],
+                    axis=1))
+            out_ref[0, c] = jnp.concatenate(rows, axis=0)
+
+
+def _layer_kernel(cols_ref, counts_ref, grp_ref, adj_ref, xc_ref, deg_ref, ws_ref, wn_ref, b_ref,
+                  *rest, per_tile, tile, n_table, n_grp, dev_blocks):
+    pieces = rest[:n_grp + 1]
+    out_ref, table_ref, sems, acc_ref, perm_ref, pick_ref = rest[n_grp + 1:]
+    r = pl.program_id(0)
+    count = counts_ref[r]
+    g = grp_ref[0]
+    part = n_grp * dev_blocks
+
+    @pl.when(r == 0)
+    def _():
         ri = lax.broadcasted_iota(jnp.int32, (tile, tile), 0)
         ci = lax.broadcasted_iota(jnp.int32, (tile, tile), 1)
         kq = tile // 8
@@ -44,24 +72,10 @@
         for cp in copies:
             cp.wait()
 
-    kk = tile // 8
-    for k in range(kk):
-        words_ref[pl.ds(k * per_tile, per_tile), :] = adj_ref[0, :, pl.ds(k * tile, tile)]
     acc_ref[...] = jnp.zeros_like(acc_ref)
 
     def chunk(c, masked):
-            words = jnp.concatenate(
-                [words_ref[pl.ds(c * CHUNK + tl, kk, stride=per_tile), :] for tl in range(CHUNK)],
-                axis=0)
-            spread = jnp.dot(words.astype(jnp.bfloat16), mexp_ref[...],
-                             preferred_element_type=jnp.float32)
-            bits = (spread.astype(jnp.int32) & 128).astype(jnp.bfloat16)
-            rows = []
-            for s in range(8):
-                rows.append(jnp.concatenate(
-                    [bits[tl * kk:(tl + 1) * kk, s * tile:(s + 1) * tile] for tl in range(CHUNK)],
-                    axis=1))
-            a_cat = jnp.concatenate(rows, axis=0)
+            a_cat = adj_ref[0, c]
             xs = []
             for tl in range(CHUNK):
                 t = c * CHUNK + tl
@@ -119,11 +133,30 @@
     spread_out = jnp.broadcast_to(chosen[None], (n_dev,) + chosen.shape).reshape(
         (n_dev * chosen.shape[0],) + chosen.shape[1:])
     halo_blocks = lax.all_to_all(spread_out, ("dom", "grp"), 0, 0, tiled=True)
+    n_chunk = per_tile // CHUNK
+    bits_call = pl.pallas_call(
+        functools.partial(_bits_kernel, per_tile=per_tile, tile=tile_rows),
+        grid_spec=pltpu.PrefetchScalarGridSpec(
+            num_scalar_prefetch=1,
+            grid=(row_blocks,),
+            in_specs=[pl.BlockSpec((1, per_tile, tile_rows * kk), lambda r, *_: (r, 0, 0))],
+            out_specs=pl.BlockSpec((1, n_chunk, tile_rows, CHUNK * tile_rows),
+                                   lambda r, *_: (r, 0, 0, 0)),
+            scratch_shapes=[pltpu.VMEM((per_tile * kk, tile_rows), jnp.int32),
+                            pltpu.VMEM((tile_rows, 8 * tile_rows), jnp.bfloat16)],
+        ),
+        out_shape=jax.ShapeDtypeStruct((row_blocks, n_chunk, tile_rows, CHUNK * tile_rows),
+                                       jnp.bfloat16),
+        compiler_params=pltpu.CompilerParams(
+            dimension_semantics=("arbitrary",), vmem_limit_bytes=32 * 1024 * 1024),
+    )
+    abits = bits_call(tile_count, adjacency)
     own_blocks = x_current.reshape(row_blocks, tile_rows, width)
     pieces = [own_blocks]
     if n_grp == 4:
         near = lax.ppermute(own_blocks, "grp", [(i, i ^ 1) for i in range(4)])
         far = lax.ppermute(own_blocks, "grp", [(i, i ^ 2) for i in range(4)])
+        far, abits = lax.optimization_barrier((far, abits))
         far_near = lax.ppermute(far, "grp", [(i, i ^ 1) for i in range(4)])
         pieces += [near, far, far_near]
     else:
@@ -136,13 +169,14 @@
     deg = degree.reshape(row_blocks, tile_rows)
     b2 = bias.reshape(1, hidden)
 
+
     kernel = functools.partial(_layer_kernel, per_tile=per_tile, tile=tile_rows, n_table=n_table,
                                n_grp=n_grp, dev_blocks=row_blocks)
     grid_spec = pltpu.PrefetchScalarGridSpec(
         num_scalar_prefetch=3,
         grid=(row_blocks,),
         in_specs=[
-            pl.BlockSpec((1, per_tile, tile_rows * kk), lambda r, *_: (r, 0, 0)),
+            pl.BlockSpec((1, n_chunk, tile_rows, CHUNK * tile_rows), lambda r, *_: (r, 0, 0, 0)),
             pl.BlockSpec((tile_rows, width), lambda r, *_: (r, 0)),
             pl.BlockSpec((row_blocks, tile_rows), lambda r, *_: (0, 0)),
             pl.BlockSpec((width, hidden), lambda r, *_: (0, 0)),
@@ -152,9 +186,7 @@
         out_specs=pl.BlockSpec((tile_rows, hidden), lambda r, *_: (r, 0)),
         scratch_shapes=[pltpu.VMEM((n_table, tile_rows, width), jnp.bfloat16),
                         pltpu.SemaphoreType.DMA((n_grp + 1,)),
-                        pltpu.VMEM((per_tile * kk, tile_rows), jnp.int32),
                         pltpu.VMEM((tile_rows, width), jnp.float32),
-                        pltpu.VMEM((tile_rows, 8 * tile_rows), jnp.bfloat16),
                         pltpu.VMEM((tile_rows, tile_rows), jnp.bfloat16),
                         pltpu.VMEM((tile_rows, tile_rows), jnp.float32)],
     )
@@ -165,7 +197,7 @@
         compiler_params=pltpu.CompilerParams(
             dimension_semantics=("arbitrary",), vmem_limit_bytes=48 * 1024 * 1024),
     )(*[pltpu.with_memory_space_constraint(a, pltpu.HBM) for a in
-        (tile_columns, tile_count, grp_idx, adjacency, x_current, deg, w_self, w_neigh, b2)], *pieces)
+        (tile_columns, tile_count, grp_idx, abits, x_current, deg, w_self, w_neigh, b2)], *pieces)
 
 
 def solution(mesh):

time: 108 us -> 110 us (1.019)
  the two profiles are of different devices: /device:TPU:7 before, /device:TPU:5 now
where the time goes in v1:
time: 110 us
  Pallas kernels  93.1 us (85%)
  starting transfers between devices  6.85 us (6%)
  local copies, waits for them, and re-layouts  6.34 us (6%)
  waiting for transfers between devices  2.15 us (2%)
    pallas_call x1, Pallas kernels, on_device(): pl.pallas_call(kernel, grid_spec=grid_spec, out_shape=jax.ShapeDtypeStruc...  56.6 us
    pallas_call x1, Pallas kernels, on_device(): abits = bits_call(tile_count, adjacency)  36.4 us
    all_to_all x1, starting transfers between devices, on_device(): halo_blocks = lax.all_to_all(spread_out, ('dom', 'grp'), 0, 0, tiled=True)  6.38 us
    unnamed x6, local copies, waits for them, and re-layouts  5.13 us
  transfers between devices with their start and end apart: 4, of which 1 were waited for; matrix products, arithmetic and copies ran while one was open for 2% of the time, Pallas kernels for 33%

profile of v1, /device:TPU:5, one launch (start us, length us, event | category | flops | bytes accessed | tf_op | source)
XLA Modules:
  0.0 109.8 jit_solution(915430879176347662)
XLA Ops:
  0.0 0.0 copy-start
  0.0 0.0 collective-permute-start
  0.8 0.5 copy-done
  1.2 1.2 %reshape.22 = bf16[32,128,128]{2,1,0:T(8,128)(2,1)} broadcast(bf16[128,128]{1,0:T(8,128)(2,1)S(1)} %dynamic-slice_bitcast_fusion), dimensions={1,2} | broadcast | bytes 1081344 | tf_op jit(solution)/shard_map/reshape | solution.py:133
  2.5 6.4 %all-to-all-start = ((bf16[32,128,128]{2,1,0:T(8,128)(2,1)}), bf16[32,128,128]{2,1,0:T(8,128)(2,1)S(1)}, u32[]{:S(2)}, u32[]{:S(2)}) async-start(bf16[32,128,128]{2,1,0:T(8,128)(2,1)} %reshape.22), calls=%async_computation | async-start | bytes 2097152 | tf_op jit(solution)/shard_map/all_to_all | solution.py:135
  8.8 0.5 collective-permute-start.1
  9.3 0.0 copy-start.1
  9.3 4.0 %copy-done.1 = s32[32,40,2048]{2,1,0:T(8,128)S(1)} copy-done((s32[32,40,2048]{2,1,0:T(8,128)S(1)}, s32[32,40,2048]{2,1,0:T(8,128)}, u32[]{:S(2)}) %copy-start.1) | copy-done | bytes 10485784
  13.3 0.0 copy-start.2
  13.3 0.7 copy-done.2
  13.9 36.4 %shard_map.100.adj_ref = bf16[32,5,128,1024]{3,2,1,0:T(8,128)(2,1)} custom-call(s32[32]{0:T(128)S(1)} %copy-done.2, s32[32,40,2048]{2,1,0:T(8,128)S(1)} %copy-done.1), custom_call_target="tpu_custom_call" | custom-call | tf_op jit(solution)/shard_map/pallas_call | solution.py:153
  50.4 0.0 collective-permute-done.rest_2_
  50.4 0.0 collective-permute-start.2
  50.4 0.6 pad_add_fusion.grp_ref
  51.0 0.0 collective-permute-done.1.rest_1_
  51.0 0.0 all-to-all-done.rest_4_
  51.0 2.1 %collective-permute-done.2.rest_3_ = bf16[32,128,128]{2,1,0:T(8,128)(2,1)} collective-permute-done((bf16[32,128,128]{2,1,0:T(8,128)(2,1)S(1)}, bf16[32,128,128]{2,1,0:T(8,128)(2,1)}, u32[]{:S(2)}, u32[]{:S(2)}) %collective-permute-start.2) | collective-permute-done | bytes 1048608 | tf_op jit(solution)/shard_map/ppermute | solution.py:160
  53.2 56.6 %shard_map.101 = bf16[4096,512]{1,0:T(8,128)(2,1)} custom-call(s32[32,40]{1,0:T(8,128)} %cols_ref.1, s32[32]{0:T(128)} %counts_ref.3, s32[2]{0:T(128)} %pad_add_fusion.grp_ref, bf16[32,5,128,1024]{3,2,1,0:T(8,128)(2,1)} %shard_map.100.adj_ref, bf16[4096,128]{1,0:T(8,128)(2,1)} %xc_ref.1, s32[32,128]{1,0:T(8,128)} %bitcast.16, bf16[128,512]{1,0:T(8,128)(2,1)} %ws_ref.1, ...), custom_call_target="tpu_custom_call" | custom-call | tf_op jit(solution)/shard_map/pallas_call | solution.py:193
  (1 shorter events, 0.0 us)
Async XLA Ops:
  0.0 1.2 %copy-start = (bf16[4096,128]{1,0:T(8,128)(2,1)S(1)}, bf16[4096,128]{1,0:T(8,128)(2,1)}, u32[]{:S(2)}) copy-start(bf16[4096,128]{1,0:T(8,128)(2,1)} %param.11) | copy-start | bytes 3145732
  0.0 50.4 %collective-permute-start = (bf16[32,128,128]{2,1,0:T(8,128)(2,1)}, bf16[32,128,128]{2,1,0:T(8,128)(2,1)S(1)}, u32[]{:S(2)}, u32[]{:S(2)}) collective-permute-start(bf16[32,128,128]{2,1,0:T(8,128)(2,1)} %bitcast.13), channel_id=1, source_target_pairs={{0,2},{1,3},{2,0},{3,1},{4,6},{5,7},{6,4},{7,5},{8,10},{9,11},{10,... | collective-permute-start | bytes 3145736 | tf_op jit(solution)/shard_map/ppermute | solution.py:158
  2.5 48.6 %all-to-all-start = ((bf16[32,128,128]{2,1,0:T(8,128)(2,1)}), bf16[32,128,128]{2,1,0:T(8,128)(2,1)S(1)}, u32[]{:S(2)}, u32[]{:S(2)}) async-start(bf16[32,128,128]{2,1,0:T(8,128)(2,1)} %reshape.22), calls=%async_computation | async-start | bytes 2097152 | tf_op jit(solution)/shard_map/all_to_all | solution.py:135
  8.8 42.2 %collective-permute-start.1 = (bf16[32,128,128]{2,1,0:T(8,128)(2,1)}, bf16[32,128,128]{2,1,0:T(8,128)(2,1)}, u32[]{:S(2)}, u32[]{:S(2)}) collective-permute-start(bf16[32,128,128]{2,1,0:T(8,128)(2,1)} %bitcast.14), channel_id=1, source_target_pairs={{0,1},{1,0},{2,3},{3,2},{4,5},{5,4},{6,7},{7,6},{8,9},{9,8},{10,11... | collective-permute-start | bytes 3145736 | tf_op jit(solution)/shard_map/ppermute | solution.py:157
  9.3 4.0 %copy-start.1 = (s32[32,40,2048]{2,1,0:T(8,128)S(1)}, s32[32,40,2048]{2,1,0:T(8,128)}, u32[]{:S(2)}) copy-start(s32[32,40,2048]{2,1,0:T(8,128)} %adj_ref.1) | copy-start | bytes 31457284
  13.3 0.7 copy-start.2
  50.4 2.8 %collective-permute-start.2 = (bf16[32,128,128]{2,1,0:T(8,128)(2,1)S(1)}, bf16[32,128,128]{2,1,0:T(8,128)(2,1)}, u32[]{:S(2)}, u32[]{:S(2)}) collective-permute-start(bf16[32,128,128]{2,1,0:T(8,128)(2,1)S(1)} %collective-permute-done.rest_2_), channel_id=1, source_target_pairs={{0,1},{1,0},{2,3},{3,2},{4,5},{5,4},{6,7},{7,6},{8,9},{9,8},{10,11... | collective-permute-start | bytes 3145736 | tf_op jit(solution)/shard_map/ppermute | solution.py:160
